TPU v7x, 256 devices: a whole 4x4x8 slice. The times are simulated.
256 devices in a mesh: scene: 16 (over y, z_hi), seq: 16 (over z_lo, x, core).
Axes of the slice: x: 4, y: 4, z: 8 (z_hi: 4, z_lo: 2; z = z_hi * 2 + z_lo), core: 2. Of those that a mesh axis runs over, the one named last changes fastest.
Arguments:
- scene_x: bfloat16 [16, 65536, 256], P('scene', 'seq'), may hold values from -6 to 6
- cotangent: bfloat16 [16, 65536, 256], P('scene', 'seq'), may hold values from -6 to 6
- gate_gain: float32 [256], replicated, may hold values from 0.3 to 3
- kernel: bfloat16 [256, 256, 256], P(None, 'seq'), may hold values from -6 to 6
- block_mix: bfloat16 [256, 256], replicated, may hold values from -0.375 to 0.375
- across_mix: bfloat16 [256, 256], replicated, may hold values from -0.375 to 0.375
- across_unmix: bfloat16 [256, 256], replicated, may hold values from -0.375 to 0.375
- block_unmix: bfloat16 [256, 256], replicated, may hold values from -0.375 to 0.375
Outputs:
- mixed: bfloat16 [16, 65536, 256], P('scene', 'seq')
- grad_x: bfloat16 [16, 65536, 256], P('scene', 'seq')
- grad_kernel: float32 [256, 256, 256], P('scene', 'seq')
- grad_gain: float32 [256], replicated
All inputs are finite; a program needn't handle non-finite values.
Results may differ from a plain program's by a relative error of at most 0.007.
Values may be sent and summed in bfloat16 or wider, within the bound.
No kernel may reach another device: no remote copies, remote signals or barrier semaphores. Data moves between devices by JAX's collectives and lax.ppermute only.
A program may use at most 128 MiB of HBM per device.

v0:
```python
import jax
import jax.numpy as jnp
from jax import lax
from jax.sharding import PartitionSpec as P


def on_device(
    scene_x, cotangent, gate_gain, kernel, block_mix, across_mix, across_unmix, block_unmix
):
    f32 = jnp.float32
    bf16 = jnp.bfloat16
    scenes_here, row_count, channels = scene_x.shape
    block_len = block_mix.shape[0]
    local_a = row_count // block_len
    kernel_f = kernel.astype(f32)
    inputs = scene_x.reshape(scenes_here, local_a, block_len, channels)
    first_mix = jnp.einsum("jb,sabc->sajc", block_mix, inputs, preferred_element_type=f32).astype(
        bf16
    )
    spread_mix = lax.all_to_all(first_mix, "seq", split_axis=2, concat_axis=1, tiled=True)
    second_mix = jnp.einsum(
        "ia,sajc->sijc", across_mix, spread_mix, preferred_element_type=f32
    ).astype(bf16)
    weighted = (second_mix.astype(f32) * kernel_f).astype(bf16)
    unmixed = jnp.einsum(
        "pi,sijc->spjc", across_unmix, weighted, preferred_element_type=f32
    ).astype(bf16)
    returned = lax.all_to_all(unmixed, "seq", split_axis=1, concat_axis=2, tiled=True)
    values = jnp.einsum("qj,spjc->spqc", block_unmix, returned, preferred_element_type=f32)
    gate_pre = inputs.astype(f32) * gate_gain
    gate_sig = jax.nn.sigmoid(gate_pre)
    mixed_out = (
        (values * gate_pre * gate_sig).astype(bf16).reshape(scenes_here, row_count, channels)
    )
    upstream = cotangent.reshape(scenes_here, local_a, block_len, channels).astype(f32)
    grad_values = (upstream * gate_pre * gate_sig).astype(bf16)
    grad_gate = upstream * values * gate_sig * (1.0 + gate_pre * (1.0 - gate_sig))
    grad_unmixed = jnp.einsum(
        "qj,spqc->spjc", block_unmix, grad_values, preferred_element_type=f32
    ).astype(bf16)
    spread_grad = lax.all_to_all(grad_unmixed, "seq", split_axis=2, concat_axis=1, tiled=True)
    grad_weighted = jnp.einsum(
        "pi,spjc->sijc", across_unmix, spread_grad, preferred_element_type=f32
    )
    kernel_term = jnp.sum(grad_weighted * second_mix.astype(f32), axis=0)
    kernel_grad = lax.psum_scatter(kernel_term, "scene", scatter_dimension=0, tiled=True)
    grad_second = (grad_weighted * kernel_f).astype(bf16)
    grad_first = jnp.einsum(
        "ia,sijc->sajc", across_mix, grad_second, preferred_element_type=f32
    ).astype(bf16)
    grad_back = lax.all_to_all(grad_first, "seq", split_axis=1, concat_axis=2, tiled=True)
    grad_input = (
        jnp.einsum("jb,sajc->sabc", block_mix, grad_back, preferred_element_type=f32)
        + grad_gate * gate_gain
    )
    grad_input = grad_input.astype(bf16).reshape(scenes_here, row_count, channels)
    gain_term = jnp.sum(inputs.astype(f32) * grad_gate, axis=(0, 1, 2))
    gain_total = lax.psum(gain_term, ("scene", "seq"))
    total_rows = scenes_here * lax.axis_size("scene") * local_a * lax.axis_size("seq") * block_len
    grad_scale = 1.0 / jnp.sqrt(jnp.float32(total_rows))
    return (mixed_out, grad_input, kernel_grad, gain_total * grad_scale)


def solution(mesh):
    return jax.shard_map(
        on_device,
        mesh=mesh,
        in_specs=(
            P("scene", "seq", None),
            P("scene", "seq", None),
            P(),
            P(None, "seq", None),
            P(),
            P(),
            P(),
            P(),
        ),
        out_specs=(P("scene", "seq", None), P("scene", "seq", None), P("scene", "seq", None), P()),
        check_vma=False,
    )
```

profile of v0, /device:TPU:1, one launch (start us, length us, event | category | flops | bytes accessed | tf_op | source)
XLA Modules:
  0.0 281.6 jit_solution(17763689708020302896)
XLA Ops:
  7.2 2.4 convert_bitcast_fusion.4
  9.6 3.1 %copy.39 = bf16[1,16,256,256]{3,1,0,2:T(8,128)(2,1)} copy(bf16[1,16,256,256]{2,3,1,0:T(8,128)(2,1)S(1)} %convert_bitcast_fusion.4) | data formatting | bytes 4194304 | tf_op jit(solution)/shard_map/convert_element_type | solution.py:17
  12.6 7.5 %all-to-all-start = ((bf16[1,16,256,256]{3,1,0,2:T(8,128)(2,1)}), bf16[1,16,256,256]{3,1,0,2:T(8,128)(2,1)}, u32[]{:S(2)}, u32[]{:S(2)}) async-start(bf16[1,16,256,256]{3,1,0,2:T(8,128)(2,1)} %copy.39), calls=%async_computation | async-start | bytes 4194304 | tf_op jit(solution)/shard_map/all_to_all | solution.py:20
  20.2 2.4 copy.46
  22.5 3.9 %convert_element_type.152 = f32[1,4096,256]{2,1,0:T(8,128)} convert(bf16[1,4096,256]{2,1,0:T(8,128)(2,1)} %param.9) | non-fusion elementwise | flops 1048576 | bytes 6291456 | tf_op jit(solution)/shard_map/convert_element_type | solution.py:35
  26.4 5.5 %copy.47 = f32[16,256,256]{1,2,0:T(8,128)} copy(f32[16,256,256]{2,1,0:T(8,128)} %bitcast.143) | data formatting | bytes 8388608 | tf_op jit(solution)/shard_map/convert_element_type | solution.py:35
  32.0 4.9 %convert_bitcast_fusion.2 = bf16[1,16,256,256]{2,3,1,0:T(8,128)(2,1)} fusion(f32[16,256,256]{1,2,0:T(8,128)} %copy.47, bf16[16,256,256]{1,2,0:T(8,128)(2,1)S(1)} %copy-done.10, f32[256]{0:T(256)S(1)} %copy-done.14, bf16[256,256]{1,0:T(8,128)(2,1)S(1)} %copy-done), kind=kOutput, calls=%fused_computation.37 | convolution fusion | flops 546308096 | bytes 8520704 | tf_op jit(solution)/shard_map/qj,spqc->spjc/dot_general | solution.py:38
  36.9 4.6 %copy.48 = bf16[1,16,256,256]{3,1,0,2:T(8,128)(2,1)} copy(bf16[1,16,256,256]{2,3,1,0:T(8,128)(2,1)} %convert_bitcast_fusion.2) | data formatting | bytes 4194304 | tf_op jit(solution)/shard_map/convert_element_type | solution.py:40
  41.5 6.5 %all-to-all-done = bf16[1,16,256,256]{3,1,0,2:T(8,128)(2,1)} async-done(((bf16[1,16,256,256]{3,1,0,2:T(8,128)(2,1)}), bf16[1,16,256,256]{3,1,0,2:T(8,128)(2,1)}, u32[]{:S(2)}, u32[]{:S(2)}) %all-to-all-start) | async-done | bytes 2097184 | tf_op jit(solution)/shard_map/all_to_all | solution.py:20
  48.0 6.0 %all-to-all-start.2 = ((bf16[1,16,256,256]{3,1,0,2:T(8,128)(2,1)}), bf16[1,16,256,256]{3,1,0,2:T(8,128)(2,1)}, u32[]{:S(2)}, u32[]{:S(2)}) async-start(bf16[1,16,256,256]{3,1,0,2:T(8,128)(2,1)} %copy.48), calls=%async_computation.2 | async-start | bytes 4194304 | tf_op jit(solution)/shard_map/all_to_all | solution.py:41
  54.0 2.7 copy.43
  56.7 2.3 copy.40
  61.6 2.1 convert_bitcast_fusion.3
  63.8 4.6 %copy.44 = bf16[1,256,16,256]{3,2,0,1:T(8,128)(2,1)} copy(bf16[1,256,16,256]{1,3,2,0:T(8,128)(2,1)} %convert_bitcast_fusion.3) | data formatting | bytes 4194304 | tf_op jit(solution)/shard_map/convert_element_type | solution.py:27
  68.3 13.4 %all-to-all-done.2 = bf16[1,16,256,256]{3,1,0,2:T(8,128)(2,1)} async-done(((bf16[1,16,256,256]{3,1,0,2:T(8,128)(2,1)}), bf16[1,16,256,256]{3,1,0,2:T(8,128)(2,1)}, u32[]{:S(2)}, u32[]{:S(2)}) %all-to-all-start.2) | async-done | bytes 2097184 | tf_op jit(solution)/shard_map/all_to_all | solution.py:41
  81.7 6.3 %all-to-all-start.1 = ((bf16[1,256,16,256]{3,2,0,1:T(8,128)(2,1)}), bf16[1,256,16,256]{3,2,0,1:T(8,128)(2,1)}, u32[]{:S(2)}, u32[]{:S(2)}) async-start(bf16[1,256,16,256]{3,2,0,1:T(8,128)(2,1)} %copy.44), calls=%async_computation.1 | async-start | bytes 4194304 | tf_op jit(solution)/shard_map/all_to_all | solution.py:28
  88.2 2.3 copy.49
  90.7 1.7 fusion.26
  92.4 2.0 copy-done.1
  94.4 2.5 fusion.15
  96.8 5.5 %copy.55 = f32[256,16,256]{2,1,0:T(8,128)} copy(f32[256,16,256]{0,2,1:T(8,128)} %fusion.15) | data formatting | bytes 8388608 | tf_op jit(solution)/shard_map/reduce_sum | solution.py:45
  103.9 4.2 %convert_bitcast_fusion.1 = bf16[1,256,16,256]{1,3,2,0:T(8,128)(2,1)} fusion(f32[16,256,256]{2,1,0:T(8,128)} %copy-done.1, bf16[256,16,256]{0,2,1:T(8,128)(2,1)S(1)} %copy-done.5, bf16[256,256]{1,0:T(8,128)(2,1)S(1)} %copy-done.11), kind=kOutput, calls=%fused_computation.36 | convolution fusion | flops 541065216 | bytes 8519680 | tf_op jit(solution)/shard_map/ia,sijc->sajc/dot_general | solution.py:48
  108.1 4.5 %copy.52 = bf16[1,256,16,256]{3,2,0,1:T(8,128)(2,1)} copy(bf16[1,256,16,256]{1,3,2,0:T(8,128)(2,1)} %convert_bitcast_fusion.1) | data formatting | bytes 4194304 | tf_op jit(solution)/shard_map/convert_element_type | solution.py:50
  112.6 3.0 %all-to-all-done.1 = bf16[1,256,16,256]{3,2,0,1:T(8,128)(2,1)} async-done(((bf16[1,256,16,256]{3,2,0,1:T(8,128)(2,1)}), bf16[1,256,16,256]{3,2,0,1:T(8,128)(2,1)}, u32[]{:S(2)}, u32[]{:S(2)}) %all-to-all-start.1) | async-done | bytes 2097184 | tf_op jit(solution)/shard_map/all_to_all | solution.py:28
  115.7 6.3 %all-to-all-start.3 = ((bf16[1,256,16,256]{3,2,0,1:T(8,128)(2,1)}), bf16[1,256,16,256]{3,2,0,1:T(8,128)(2,1)S(1)}, u32[]{:S(2)}, u32[]{:S(2)}) async-start(bf16[1,256,16,256]{3,2,0,1:T(8,128)(2,1)} %copy.52), calls=%async_computation.3 | async-start | bytes 4194304 | tf_op jit(solution)/shard_map/all_to_all | solution.py:51
  121.9 3.2 %copy.45 = bf16[1,16,16,16,256]{4,3,2,1,0:T(8,128)(2,1)} copy(bf16[1,16,16,16,256]{4,3,1,2,0:T(8,128)(2,1)} %bitcast.16) | data formatting | bytes 4194304 | tf_op jit(solution)/shard_map/all_to_all | solution.py:28
  125.1 54.0 %all-to-all-done.3 = bf16[1,256,16,256]{3,2,0,1:T(8,128)(2,1)S(1)} async-done(((bf16[1,256,16,256]{3,2,0,1:T(8,128)(2,1)}), bf16[1,256,16,256]{3,2,0,1:T(8,128)(2,1)S(1)}, u32[]{:S(2)}, u32[]{:S(2)}) %all-to-all-start.3) | async-done | bytes 2097184 | tf_op jit(solution)/shard_map/all_to_all | solution.py:51
  180.4 2.0 copy.53
  183.3 5.0 %fusion.11 = (f32[1,16,256,256]{3,2,1,0:T(8,128)S(1)}, bf16[1,16,256,256]{3,2,1,0:T(8,128)(2,1)}) fusion(f32[1,16,256,256]{3,2,1,0:T(8,128)} %bitcast.144, f32[256]{0:T(256)S(1)} %copy-done.14, bf16[1,4096,256]{2,1,0:T(8,128)(2,1)S(1)} %copy-done.3, bf16[16,256,256]{2,1,0:T(8,128)(2,1)S(1)} %bitcast.152, bf16[256,256]{1,0:T(8,128)(2,1)S(1)} %copy-done), kind=kOutput, calls=%fused_computation.15 | convolution fusion | flops 551550976 | bytes 14812160 | tf_op jit(solution)/shard_map/qj,spjc->spqc/dot_general | solution.py:29
  188.3 2.0 copy-done.6
  190.9 78.8 %psum.7 = f32[256]{0:T(256)S(1)} all-reduce(f32[256]{0:T(256)S(1)} %fusion.12), channel_id=1, replica_groups=mesh['scene'=16,'seq'=16] {'scene','seq'}, use_global_device_ids=true, to_apply=%region_2.0 | all-reduce | flops 256 | bytes 2048 | tf_op jit(solution)/shard_map/psum | solution.py:58
  270.3 4.5 %fusion.13 = bf16[1,16,256,256]{3,2,1,0:T(8,128)(2,1)} fusion(f32[1,16,256,256]{3,2,1,0:T(8,128)} %copy-done.6, bf16[16,256,256]{2,1,0:T(8,128)(2,1)S(1)} %bitcast.145, f32[256]{0:T(256)S(1)} %copy-done.14, bf16[256,256]{1,0:T(8,128)(2,1)S(1)} %copy-done.12), kind=kOutput, calls=%fused_computation.18 | convolution fusion | flops 540016640 | bytes 8520704 | tf_op jit(solution)/shard_map/jb,sajc->sabc/dot_general | solution.py:53
  (36 shorter events, 8.1 us)
Async XLA Ops:
  7.2 24.8 %copy-start = (bf16[256,256]{1,0:T(8,128)(2,1)S(1)}, bf16[256,256]{1,0:T(8,128)(2,1)}, u32[]{:S(2)}) copy-start(bf16[256,256]{1,0:T(8,128)(2,1)} %param.15) | copy-start | bytes 393220
  12.6 7.5 %copy-start.2 = (bf16[1,4096,256]{2,1,0:T(8,128)(2,1)S(1)}, bf16[1,4096,256]{2,1,0:T(8,128)(2,1)}, u32[]{:S(2)}) copy-start(bf16[1,4096,256]{2,1,0:T(8,128)(2,1)} %param.8) | copy-start | bytes 6291460
  12.6 35.3 %all-to-all-start = ((bf16[1,16,256,256]{3,1,0,2:T(8,128)(2,1)}), bf16[1,16,256,256]{3,1,0,2:T(8,128)(2,1)}, u32[]{:S(2)}, u32[]{:S(2)}) async-start(bf16[1,16,256,256]{3,1,0,2:T(8,128)(2,1)} %copy.39), calls=%async_computation | async-start | bytes 4194304 | tf_op jit(solution)/shard_map/all_to_all | solution.py:20
  26.4 5.6 %copy-start.10 = (bf16[16,256,256]{1,2,0:T(8,128)(2,1)S(1)}, bf16[16,256,256]{1,2,0:T(8,128)(2,1)}, u32[]{:S(2)}) copy-start(bf16[16,256,256]{1,2,0:T(8,128)(2,1)} %copy.46) | copy-start | bytes 6291460
  26.4 5.6 %copy-start.14 = (f32[256]{0:T(256)S(1)}, f32[256]{0:T(256)}, u32[]{:S(2)}) copy-start(f32[256]{0:T(256)} %param.10) | copy-start | bytes 3076
  41.5 12.5 %copy-start.8 = (bf16[256,16,256]{2,1,0:T(8,128)(2,1)S(1)}, bf16[256,16,256]{2,1,0:T(8,128)(2,1)}, u32[]{:S(2)}) copy-start(bf16[256,16,256]{2,1,0:T(8,128)(2,1)} %param.11) | copy-start | bytes 6291460
  48.0 33.7 %all-to-all-start.2 = ((bf16[1,16,256,256]{3,1,0,2:T(8,128)(2,1)}), bf16[1,16,256,256]{3,1,0,2:T(8,128)(2,1)}, u32[]{:S(2)}, u32[]{:S(2)}) async-start(bf16[1,16,256,256]{3,1,0,2:T(8,128)(2,1)} %copy.48), calls=%async_computation.2 | async-start | bytes 4194304 | tf_op jit(solution)/shard_map/all_to_all | solution.py:41
  59.0 0.9 copy-start.11
  59.9 1.7 copy-start.4
  60.0 1.7 copy-start.13
  81.7 34.0 %all-to-all-start.1 = ((bf16[1,256,16,256]{3,2,0,1:T(8,128)(2,1)}), bf16[1,256,16,256]{3,2,0,1:T(8,128)(2,1)}, u32[]{:S(2)}, u32[]{:S(2)}) async-start(bf16[1,256,16,256]{3,2,0,1:T(8,128)(2,1)} %copy.44), calls=%async_computation.1 | async-start | bytes 4194304 | tf_op jit(solution)/shard_map/all_to_all | solution.py:28
  88.0 186.8 %reduce-scatter.2.cloned.1.call-start = ((), (), s32[]{:S(2)}) async-start(), calls=%async_computation.5 | async-start | bytes 4456448 | tf_op jit(solution)/shard_map/reduce_scatter | solution.py:46
  92.4 2.0 copy-start.1
  102.3 1.6 copy-start.5
  115.7 63.4 %all-to-all-start.3 = ((bf16[1,256,16,256]{3,2,0,1:T(8,128)(2,1)}), bf16[1,256,16,256]{3,2,0,1:T(8,128)(2,1)S(1)}, u32[]{:S(2)}, u32[]{:S(2)}) async-start(bf16[1,256,16,256]{3,2,0,1:T(8,128)(2,1)} %copy.52), calls=%async_computation.3 | async-start | bytes 4194304 | tf_op jit(solution)/shard_map/all_to_all | solution.py:51
  179.1 1.3 copy-start.7
  180.4 2.2 copy-start.3
  180.4 2.9 %copy-start.9 = (bf16[1,16,16,16,256]{4,3,2,1,0:T(8,128)(2,1)S(1)}, bf16[1,16,16,16,256]{4,3,2,1,0:T(8,128)(2,1)}, u32[]{:S(2)}) copy-start(bf16[1,16,16,16,256]{4,3,2,1,0:T(8,128)(2,1)} %copy.45) | copy-start | bytes 6291460
  188.3 2.0 copy-start.6
  190.2 80.1 %copy-start.12 = (bf16[256,256]{1,0:T(8,128)(2,1)S(1)}, bf16[256,256]{1,0:T(8,128)(2,1)}, u32[]{:S(2)}) copy-start(bf16[256,256]{1,0:T(8,128)(2,1)} %param.12) | copy-start | bytes 393220
Sparse Core Ops, SparseCore 0:
  102.5 100.8 reduce-scatter.1
where the time goes:
time: 283 us; the launch traced here: 282 us
  blocking collectives  78.8 us (28%)
  waiting for transfers between devices  76.9 us (27%)
  local copies, waits for them, and re-layouts  51.5 us (18%)
  matrix products  26.4 us (9%)
  starting transfers between devices  26.2 us (9%)
  between operations  14.2 us (5%)
  other arithmetic  7.59 us (3%)
    psum x1, blocking collectives, on_device(): gain_total = lax.psum(gain_term, ('scene', 'seq'))  78.8 us
    all_to_all x1, waiting for transfers between devices, on_device(): lax.all_to_all(grad_first, 'seq', split_axis=1, concat_axis=2, tiled=True)  54 us
    all_to_all x1, waiting for transfers between devices, on_device(): lax.all_to_all(grad_unmixed, 'seq', split_axis=2, concat_axis=1, tiled=True)  13.4 us
    unnamed x31, local copies, waits for them, and re-layouts  11.2 us
    all_to_all x1, starting transfers between devices, on_device(): lax.all_to_all(first_mix, 'seq', split_axis=2, concat_axis=1, tiled=True)  7.5 us
    all_to_all x1, waiting for transfers between devices, on_device(): lax.all_to_all(first_mix, 'seq', split_axis=2, concat_axis=1, tiled=True)  6.49 us
    all_to_all x1, starting transfers between devices, on_device(): lax.all_to_all(grad_first, 'seq', split_axis=1, concat_axis=2, tiled=True)  6.26 us
    all_to_all x1, starting transfers between devices, on_device(): lax.all_to_all(unmixed, 'seq', split_axis=1, concat_axis=2, tiled=True)  6.26 us
  transfers between devices with their start and end apart: 5, of which 4 were waited for; matrix products, arithmetic and copies ran while one was open for 25% of the time, Pallas kernels for 0%

commit v1 on v0

--- a/solution.py
+++ b/solution.py
@@ -55,7 +55,7 @@
     )
     grad_input = grad_input.astype(bf16).reshape(scenes_here, row_count, channels)
     gain_term = jnp.sum(inputs.astype(f32) * grad_gate, axis=(0, 1, 2))
-    gain_total = lax.psum(gain_term, ("scene", "seq"))
+    gain_total = jnp.sum(lax.all_gather(gain_term, ("scene", "seq")), axis=0)
     total_rows = scenes_here * lax.axis_size("scene") * local_a * lax.axis_size("seq") * block_len
     grad_scale = 1.0 / jnp.sqrt(jnp.float32(total_rows))
     return (mixed_out, grad_input, kernel_grad, gain_total * grad_scale)

time: 283 us -> 268 us (0.947)
  blocking collectives: 78.8 us -> 64.2 us
    psum x1 -> x0, blocking collectives: 78.8 us -> none  [on_device(): gain_total = lax.psum(gain_term, ('scene', 'seq'))]
    all_gather x0 -> x1, blocking collectives: none -> 64.2 us  [on_device(): gain_total = jnp.sum(lax.all_gather(gain_term, ('scene', 'seq')), axis=0)]
  transfers between devices with their start and end apart: 5 -> 5, of which waited for: 4 -> 4; matrix products, arithmetic and copies ran while one was open for 25% -> 27% of each run, Pallas kernels for 0% -> 0%
where the time goes in v1:
time: 268 us; the launch traced here: 267 us
  waiting for transfers between devices  76.9 us (29%)
  blocking collectives  64.2 us (24%)
  local copies, waits for them, and re-layouts  50.8 us (19%)
  matrix products  26.4 us (10%)
  starting transfers between devices  26.2 us (10%)
  between operations  14.2 us (5%)
  other arithmetic  7.89 us (3%)
    all_gather x1, blocking collectives, on_device(): gain_total = jnp.sum(lax.all_gather(gain_term, ('scene', 'seq')), axis=0)  64.2 us
    all_to_all x1, waiting for transfers between devices, on_device(): lax.all_to_all(grad_first, 'seq', split_axis=1, concat_axis=2, tiled=True)  54 us
    all_to_all x1, waiting for transfers between devices, on_device(): lax.all_to_all(grad_unmixed, 'seq', split_axis=2, concat_axis=1, tiled=True)  13.4 us
    unnamed x31, local copies, waits for them, and re-layouts  10.4 us
    all_to_all x1, starting transfers between devices, on_device(): lax.all_to_all(first_mix, 'seq', split_axis=2, concat_axis=1, tiled=True)  7.5 us
    all_to_all x1, waiting for transfers between devices, on_device(): lax.all_to_all(first_mix, 'seq', split_axis=2, concat_axis=1, tiled=True)  6.49 us
    all_to_all x1, starting transfers between devices, on_device(): lax.all_to_all(grad_first, 'seq', split_axis=1, concat_axis=2, tiled=True)  6.26 us
    all_to_all x1, starting transfers between devices, on_device(): lax.all_to_all(unmixed, 'seq', split_axis=1, concat_axis=2, tiled=True)  6.26 us
  transfers between devices with their start and end apart: 5, of which 4 were waited for; matrix products, arithmetic and copies ran while one was open for 27% of the time, Pallas kernels for 0%

profile of v1, /device:TPU:1, one launch (start us, length us, event | category | flops | bytes accessed | tf_op | source)
XLA Modules:
  0.0 266.6 jit_solution(2077352756767768912)
XLA Ops:
  7.2 2.4 convert_bitcast_fusion.4
  9.6 3.1 %copy.39 = bf16[1,16,256,256]{3,1,0,2:T(8,128)(2,1)} copy(bf16[1,16,256,256]{2,3,1,0:T(8,128)(2,1)S(1)} %convert_bitcast_fusion.4) | data formatting | bytes 4194304 | tf_op jit(solution)/shard_map/convert_element_type | solution.py:17
  12.6 7.5 %all-to-all-start = ((bf16[1,16,256,256]{3,1,0,2:T(8,128)(2,1)}), bf16[1,16,256,256]{3,1,0,2:T(8,128)(2,1)}, u32[]{:S(2)}, u32[]{:S(2)}) async-start(bf16[1,16,256,256]{3,1,0,2:T(8,128)(2,1)} %copy.39), calls=%async_computation | async-start | bytes 4194304 | tf_op jit(solution)/shard_map/all_to_all | solution.py:20
  20.2 2.4 copy.46
  22.5 3.9 %convert_element_type.152 = f32[1,4096,256]{2,1,0:T(8,128)} convert(bf16[1,4096,256]{2,1,0:T(8,128)(2,1)} %param.9) | non-fusion elementwise | flops 1048576 | bytes 6291456 | tf_op jit(solution)/shard_map/convert_element_type | solution.py:35
  26.4 5.5 %copy.47 = f32[16,256,256]{1,2,0:T(8,128)} copy(f32[16,256,256]{2,1,0:T(8,128)} %bitcast.144) | data formatting | bytes 8388608 | tf_op jit(solution)/shard_map/convert_element_type | solution.py:35
  32.0 4.9 %convert_bitcast_fusion.2 = bf16[1,16,256,256]{2,3,1,0:T(8,128)(2,1)} fusion(f32[16,256,256]{1,2,0:T(8,128)} %copy.47, bf16[16,256,256]{1,2,0:T(8,128)(2,1)S(1)} %copy-done.10, f32[256]{0:T(256)S(1)} %copy-done.14, bf16[256,256]{1,0:T(8,128)(2,1)S(1)} %copy-done), kind=kOutput, calls=%fused_computation.37 | convolution fusion | flops 546308096 | bytes 8520704 | tf_op jit(solution)/shard_map/qj,spqc->spjc/dot_general | solution.py:38
  36.9 4.6 %copy.48 = bf16[1,16,256,256]{3,1,0,2:T(8,128)(2,1)} copy(bf16[1,16,256,256]{2,3,1,0:T(8,128)(2,1)} %convert_bitcast_fusion.2) | data formatting | bytes 4194304 | tf_op jit(solution)/shard_map/convert_element_type | solution.py:40
  41.5 6.5 %all-to-all-done = bf16[1,16,256,256]{3,1,0,2:T(8,128)(2,1)} async-done(((bf16[1,16,256,256]{3,1,0,2:T(8,128)(2,1)}), bf16[1,16,256,256]{3,1,0,2:T(8,128)(2,1)}, u32[]{:S(2)}, u32[]{:S(2)}) %all-to-all-start) | async-done | bytes 2097184 | tf_op jit(solution)/shard_map/all_to_all | solution.py:20
  48.0 6.0 %all-to-all-start.2 = ((bf16[1,16,256,256]{3,1,0,2:T(8,128)(2,1)}), bf16[1,16,256,256]{3,1,0,2:T(8,128)(2,1)}, u32[]{:S(2)}, u32[]{:S(2)}) async-start(bf16[1,16,256,256]{3,1,0,2:T(8,128)(2,1)} %copy.48), calls=%async_computation.2 | async-start | bytes 4194304 | tf_op jit(solution)/shard_map/all_to_all | solution.py:41
  54.0 2.7 %copy.43 = bf16[256,16,256]{0,2,1:T(8,128)(2,1)} copy(bf16[256,16,256]{2,1,0:T(8,128)(2,1)S(1)} %copy-done.8) | data formatting | bytes 4194304 | tf_op args[3]
  56.7 2.3 copy.40
  60.0 1.7 fusion.31
  61.6 2.1 convert_bitcast_fusion.3
  63.8 4.6 %copy.44 = bf16[1,256,16,256]{3,2,0,1:T(8,128)(2,1)} copy(bf16[1,256,16,256]{1,3,2,0:T(8,128)(2,1)} %convert_bitcast_fusion.3) | data formatting | bytes 4194304 | tf_op jit(solution)/shard_map/convert_element_type | solution.py:27
  68.3 13.4 %all-to-all-done.2 = bf16[1,16,256,256]{3,1,0,2:T(8,128)(2,1)} async-done(((bf16[1,16,256,256]{3,1,0,2:T(8,128)(2,1)}), bf16[1,16,256,256]{3,1,0,2:T(8,128)(2,1)}, u32[]{:S(2)}, u32[]{:S(2)}) %all-to-all-start.2) | async-done | bytes 2097184 | tf_op jit(solution)/shard_map/all_to_all | solution.py:41
  81.7 6.3 %all-to-all-start.1 = ((bf16[1,256,16,256]{3,2,0,1:T(8,128)(2,1)}), bf16[1,256,16,256]{3,2,0,1:T(8,128)(2,1)}, u32[]{:S(2)}, u32[]{:S(2)}) async-start(bf16[1,256,16,256]{3,2,0,1:T(8,128)(2,1)} %copy.44), calls=%async_computation.1 | async-start | bytes 4194304 | tf_op jit(solution)/shard_map/all_to_all | solution.py:28
  88.2 2.3 copy.49
  90.7 1.7 fusion.26
  92.4 2.0 copy-done.1
  94.4 2.5 fusion.15
  96.8 5.5 %copy.55 = f32[256,16,256]{2,1,0:T(8,128)} copy(f32[256,16,256]{0,2,1:T(8,128)} %fusion.15) | data formatting | bytes 8388608 | tf_op jit(solution)/shard_map/reduce_sum | solution.py:45
  103.9 4.2 %convert_bitcast_fusion.1 = bf16[1,256,16,256]{1,3,2,0:T(8,128)(2,1)} fusion(f32[16,256,256]{2,1,0:T(8,128)} %copy-done.1, bf16[256,16,256]{0,2,1:T(8,128)(2,1)S(1)} %copy-done.5, bf16[256,256]{1,0:T(8,128)(2,1)S(1)} %copy-done.11), kind=kOutput, calls=%fused_computation.36 | convolution fusion | flops 541065216 | bytes 8519680 | tf_op jit(solution)/shard_map/ia,sijc->sajc/dot_general | solution.py:48
  108.1 4.5 %copy.52 = bf16[1,256,16,256]{3,2,0,1:T(8,128)(2,1)} copy(bf16[1,256,16,256]{1,3,2,0:T(8,128)(2,1)} %convert_bitcast_fusion.1) | data formatting | bytes 4194304 | tf_op jit(solution)/shard_map/convert_element_type | solution.py:50
  112.6 3.0 %all-to-all-done.1 = bf16[1,256,16,256]{3,2,0,1:T(8,128)(2,1)} async-done(((bf16[1,256,16,256]{3,2,0,1:T(8,128)(2,1)}), bf16[1,256,16,256]{3,2,0,1:T(8,128)(2,1)}, u32[]{:S(2)}, u32[]{:S(2)}) %all-to-all-start.1) | async-done | bytes 2097184 | tf_op jit(solution)/shard_map/all_to_all | solution.py:28
  115.7 6.3 %all-to-all-start.3 = ((bf16[1,256,16,256]{3,2,0,1:T(8,128)(2,1)}), bf16[1,256,16,256]{3,2,0,1:T(8,128)(2,1)S(1)}, u32[]{:S(2)}, u32[]{:S(2)}) async-start(bf16[1,256,16,256]{3,2,0,1:T(8,128)(2,1)} %copy.52), calls=%async_computation.3 | async-start | bytes 4194304 | tf_op jit(solution)/shard_map/all_to_all | solution.py:51
  121.9 3.2 %copy.45 = bf16[1,16,16,16,256]{4,3,2,1,0:T(8,128)(2,1)} copy(bf16[1,16,16,16,256]{4,3,1,2,0:T(8,128)(2,1)} %bitcast.16) | data formatting | bytes 4194304 | tf_op jit(solution)/shard_map/all_to_all | solution.py:28
  125.1 54.0 %all-to-all-done.3 = bf16[1,256,16,256]{3,2,0,1:T(8,128)(2,1)S(1)} async-done(((bf16[1,256,16,256]{3,2,0,1:T(8,128)(2,1)}), bf16[1,256,16,256]{3,2,0,1:T(8,128)(2,1)S(1)}, u32[]{:S(2)}, u32[]{:S(2)}) %all-to-all-start.3) | async-done | bytes 2097184 | tf_op jit(solution)/shard_map/all_to_all | solution.py:51
  180.4 2.0 copy.53
  183.3 5.0 %fusion.11 = (f32[1,16,256,256]{3,2,1,0:T(8,128)S(1)}, bf16[1,16,256,256]{3,2,1,0:T(8,128)(2,1)}) fusion(f32[1,16,256,256]{3,2,1,0:T(8,128)} %bitcast.145, f32[256]{0:T(256)S(1)} %copy-done.14, bf16[1,4096,256]{2,1,0:T(8,128)(2,1)S(1)} %copy-done.3, bf16[16,256,256]{2,1,0:T(8,128)(2,1)S(1)} %bitcast.153, bf16[256,256]{1,0:T(8,128)(2,1)S(1)} %copy-done), kind=kOutput, calls=%fused_computation.15 | convolution fusion | flops 551550976 | bytes 14812160 | tf_op jit(solution)/shard_map/qj,spjc->spqc/dot_general | solution.py:29
  190.2 64.2 %all-gather.1 = f32[256,1,256]{2,1,0:T(1,128)S(1)} all-gather(f32[1,1,256]{2,1,0:T(1,128)S(1)} %bitcast.154), channel_id=2, replica_groups=mesh['scene'=16,'seq'=16] {'scene','seq'}, dimensions={0}, use_global_device_ids=true | all-gather | bytes 263168 | tf_op jit(solution)/shard_map/all_gather | solution.py:58
  255.3 4.5 %fusion.13 = bf16[1,16,256,256]{3,2,1,0:T(8,128)(2,1)} fusion(f32[1,16,256,256]{3,2,1,0:T(8,128)} %copy-done.6, bf16[16,256,256]{2,1,0:T(8,128)(2,1)S(1)} %bitcast.146, f32[256]{0:T(256)S(1)} %copy-done.14, bf16[256,256]{1,0:T(8,128)(2,1)S(1)} %copy-done.12), kind=kOutput, calls=%fused_computation.18 | convolution fusion | flops 540016640 | bytes 8520704 | tf_op jit(solution)/shard_map/jb,sajc->sabc/dot_general | solution.py:53
  (37 shorter events, 8.0 us)
Async XLA Ops:
  7.2 24.8 %copy-start = (bf16[256,256]{1,0:T(8,128)(2,1)S(1)}, bf16[256,256]{1,0:T(8,128)(2,1)}, u32[]{:S(2)}) copy-start(bf16[256,256]{1,0:T(8,128)(2,1)} %param.15) | copy-start | bytes 393220
  12.6 7.5 %copy-start.2 = (bf16[1,4096,256]{2,1,0:T(8,128)(2,1)S(1)}, bf16[1,4096,256]{2,1,0:T(8,128)(2,1)}, u32[]{:S(2)}) copy-start(bf16[1,4096,256]{2,1,0:T(8,128)(2,1)} %param.8) | copy-start | bytes 6291460
  12.6 35.3 %all-to-all-start = ((bf16[1,16,256,256]{3,1,0,2:T(8,128)(2,1)}), bf16[1,16,256,256]{3,1,0,2:T(8,128)(2,1)}, u32[]{:S(2)}, u32[]{:S(2)}) async-start(bf16[1,16,256,256]{3,1,0,2:T(8,128)(2,1)} %copy.39), calls=%async_computation | async-start | bytes 4194304 | tf_op jit(solution)/shard_map/all_to_all | solution.py:20
  26.4 5.6 %copy-start.10 = (bf16[16,256,256]{1,2,0:T(8,128)(2,1)S(1)}, bf16[16,256,256]{1,2,0:T(8,128)(2,1)}, u32[]{:S(2)}) copy-start(bf16[16,256,256]{1,2,0:T(8,128)(2,1)} %copy.46) | copy-start | bytes 6291460
  26.4 5.6 %copy-start.14 = (f32[256]{0:T(256)S(1)}, f32[256]{0:T(256)}, u32[]{:S(2)}) copy-start(f32[256]{0:T(256)} %param.10) | copy-start | bytes 3076
  41.5 12.5 %copy-start.8 = (bf16[256,16,256]{2,1,0:T(8,128)(2,1)S(1)}, bf16[256,16,256]{2,1,0:T(8,128)(2,1)}, u32[]{:S(2)}) copy-start(bf16[256,16,256]{2,1,0:T(8,128)(2,1)} %param.11) | copy-start | bytes 6291460
  48.0 33.7 %all-to-all-start.2 = ((bf16[1,16,256,256]{3,1,0,2:T(8,128)(2,1)}), bf16[1,16,256,256]{3,1,0,2:T(8,128)(2,1)}, u32[]{:S(2)}, u32[]{:S(2)}) async-start(bf16[1,16,256,256]{3,1,0,2:T(8,128)(2,1)} %copy.48), calls=%async_computation.2 | async-start | bytes 4194304 | tf_op jit(solution)/shard_map/all_to_all | solution.py:41
  59.0 0.9 copy-start.11
  59.9 1.7 copy-start.4
  60.0 1.7 copy-start.13
  81.7 34.0 %all-to-all-start.1 = ((bf16[1,256,16,256]{3,2,0,1:T(8,128)(2,1)}), bf16[1,256,16,256]{3,2,0,1:T(8,128)(2,1)}, u32[]{:S(2)}, u32[]{:S(2)}) async-start(bf16[1,256,16,256]{3,2,0,1:T(8,128)(2,1)} %copy.44), calls=%async_computation.1 | async-start | bytes 4194304 | tf_op jit(solution)/shard_map/all_to_all | solution.py:28
  88.0 171.8 %reduce-scatter.2.cloned.1.call-start = ((), (), s32[]{:S(2)}) async-start(), calls=%async_computation.5 | async-start | bytes 4456448 | tf_op jit(solution)/shard_map/reduce_scatter | solution.py:46
  92.4 2.0 copy-start.1
  102.3 1.6 copy-start.5
  115.7 63.4 %all-to-all-start.3 = ((bf16[1,256,16,256]{3,2,0,1:T(8,128)(2,1)}), bf16[1,256,16,256]{3,2,0,1:T(8,128)(2,1)S(1)}, u32[]{:S(2)}, u32[]{:S(2)}) async-start(bf16[1,256,16,256]{3,2,0,1:T(8,128)(2,1)} %copy.52), calls=%async_computation.3 | async-start | bytes 4194304 | tf_op jit(solution)/shard_map/all_to_all | solution.py:51
  179.1 1.3 copy-start.7
  180.4 2.2 copy-start.3
  180.4 2.9 %copy-start.9 = (bf16[1,16,16,16,256]{4,3,2,1,0:T(8,128)(2,1)S(1)}, bf16[1,16,16,16,256]{4,3,2,1,0:T(8,128)(2,1)}, u32[]{:S(2)}) copy-start(bf16[1,16,16,16,256]{4,3,2,1,0:T(8,128)(2,1)} %copy.45) | copy-start | bytes 6291460
  188.3 2.0 copy-start.6
  188.3 67.0 %copy-start.12 = (bf16[256,256]{1,0:T(8,128)(2,1)S(1)}, bf16[256,256]{1,0:T(8,128)(2,1)}, u32[]{:S(2)}) copy-start(bf16[256,256]{1,0:T(8,128)(2,1)} %param.12) | copy-start | bytes 393220
Sparse Core Ops, SparseCore 0:
  102.5 100.6 reduce-scatter.1
